TPU v7x, 128 devices: a whole 4x4x4 slice. The times are simulated.
128 devices in a mesh: section: 4 (over x_hi, core), dom: 32 (over z, y, x_lo).
Axes of the slice: x: 4 (x_hi: 2, x_lo: 2; x = x_hi * 2 + x_lo), y: 4, z: 4, core: 2. Of those that a mesh axis runs over, the one named last changes fastest.
Arguments:
- features: bfloat16 [4, 4096, 512], P(None, 'dom'), may hold values from -6 to 6
- adjacency: bfloat16 [4, 64, 64, 2112], P(None, 'dom'), may hold values from -0.125 to 0.125
- boundary: int32 [4, 32, 32], replicated, may hold values from 0 to 1
- layer_counts: int32 [4], P('section'), may hold values from 0 to 2, as said below
- weights: bfloat16 [4, 2, 512, 512], P('section'), may hold values from -0.25 to 0.25
Outputs:
- stashed: bfloat16 [4, 4, 4096, 512], P('section', None, 'dom')
Inputs may be any that keep to these rules, and one draw needn't show every extreme that they name: `layer_counts`: the number of layer slots that section uses; some section uses all 2 and some none. `boundary`: a local block index within the sending partition.
All inputs are finite; a program needn't handle non-finite values.
Results may differ from a plain program's by a relative error of at most 0.009.
Values may be sent and summed in bfloat16 or wider, within the bound.
No kernel may reach another device: no remote copies, remote signals or barrier semaphores. Data moves between devices by JAX's collectives and lax.ppermute only.
A program may use at most 64 MiB of HBM per device.

v0:
```python
import jax
import jax.numpy as jnp
from jax import lax
from jax.sharding import PartitionSpec as P


def shifted(value, axis, steps):
    count = lax.axis_size(axis)
    return lax.ppermute(value, axis, [(source, (source + steps) % count) for source in range(count)])


def sent_one_way(value, axis, source, target):
    return lax.ppermute(value, axis, [(source, target)])


def local(features, adjacency, boundary, layer_counts, weights):
    section_count = lax.axis_size("section")
    part_count = lax.axis_size("dom")
    group = lax.axis_index("section")
    part_here = lax.axis_index("dom")
    local_rows = features.shape[1]
    feature_width = features.shape[2]
    local_blocks = adjacency.shape[1]
    block_rows = adjacency.shape[2]
    slot_total = weights.shape[1]

    counts_shifted = [layer_counts] + [
        shifted(layer_counts, "section", step) for step in range(1, section_count)
    ]
    count_stack = jnp.concatenate(counts_shifted)
    count_by_section = count_stack[(group - jnp.arange(section_count, dtype=jnp.int32)) % section_count]
    trips = jnp.clip(count_by_section, 0, slot_total)

    hidden = lax.dynamic_index_in_dim(features, group, 0, keepdims=False)
    adj_tiles = lax.dynamic_index_in_dim(adjacency, group, 0, keepdims=False)
    bound_ids = lax.dynamic_index_in_dim(boundary, group, 0, keepdims=False)
    send_ids = bound_ids[part_here]
    local_cols = local_blocks * block_rows
    adj_t = adj_tiles.reshape(local_cols, -1).T.reshape(-1, block_rows, local_cols)
    adj_t_local = adj_t[:local_blocks].reshape(local_cols, local_cols)
    adj_t_remote = jnp.concatenate(
        [adj_t[local_blocks:], jnp.zeros((1, block_rows, local_cols), adj_t.dtype)], axis=0
    )
    slot_of_part = (jnp.arange(part_count, dtype=jnp.int32) - part_here - 1) % part_count
    adj_t_by_part = adj_t_remote[slot_of_part].reshape(part_count * block_rows, local_cols)

    def normed_of(hidden):
        local_view = hidden.reshape(local_blocks, block_rows, feature_width)
        outgoing = local_view[send_ids]
        incoming = lax.all_to_all(outgoing, "dom", 0, 0, tiled=True)
        aggregate = jnp.einsum(
            "kb,kd->bd", adj_t_local, hidden, preferred_element_type=jnp.float32
        ) + jnp.einsum(
            "kb,kd->bd", adj_t_by_part, incoming.reshape(-1, feature_width),
            preferred_element_type=jnp.float32,
        )
        mean_square = jnp.mean(aggregate * aggregate, axis=-1, keepdims=True)
        return (aggregate * lax.rsqrt(mean_square + 1e-06)).astype(jnp.bfloat16)

    def projected_onto(hidden, normed, weight):
        projected = jnp.dot(normed, weight, preferred_element_type=jnp.float32)
        return (hidden.astype(jnp.float32) + jax.nn.relu(projected)).astype(jnp.bfloat16)

    if section_count == 4:
        across = shifted(weights[0], "section", 2)
        beside = lax.ppermute(
            jnp.stack([weights[0], across]), "section", [(0, 1), (1, 0), (2, 3), (3, 2)]
        )
        weight_list = jnp.stack([weights[0], beside[0], across, beside[1]])

        def list_index(section):
            return jnp.bitwise_xor(section, group)
    else:
        weight_list = jnp.stack(
            [weights[0]] + [shifted(weights[0], "section", step) for step in range(1, section_count)]
        )

        def list_index(section):
            return (group - section) % section_count

    finished = jnp.cumsum(trips)
    total = finished[-1]

    def weight_for(layer):
        section = jnp.sum((finished <= layer).astype(jnp.int32))
        section = jnp.minimum(section, section_count - 1)
        slot = layer - (finished[section] - trips[section])
        slot = jnp.clip(slot, 0, slot_total - 1)
        chosen = lax.dynamic_index_in_dim(weight_list, list_index(section), 0, keepdims=False)
        return lax.dynamic_index_in_dim(chosen, slot, 0, keepdims=False)

    def recorded(stash, hidden, done):
        return jnp.where((finished == done)[:, None, None], hidden[None], stash)

    stash = jnp.broadcast_to(hidden[None], (section_count,) + hidden.shape)
    normed = normed_of(hidden)

    def layer_step(layer, carry):
        hidden, normed, stash = carry
        hidden = projected_onto(hidden, normed, weight_for(layer))
        stash = recorded(stash, hidden, layer + 1)
        return hidden, normed_of(hidden), stash

    hidden, normed, stash = lax.fori_loop(
        0, jnp.maximum(total - 1, 0), layer_step, (hidden, normed, stash)
    )
    last = jnp.maximum(total - 1, 0)
    hidden = projected_onto(hidden, normed, weight_for(last))
    stash = jnp.where(total >= 1, recorded(stash, hidden, total), stash)

    stash_stack = stash
    arrived = [lax.dynamic_index_in_dim(stash_stack, group, 0, keepdims=False)]
    for step in range(1, section_count):
        piece = lax.dynamic_index_in_dim(stash_stack, (group + step) % section_count, 0, keepdims=False)
        arrived.append(shifted(piece, "section", step))
    arrived = jnp.stack(arrived)
    out = arrived[(group - jnp.arange(section_count, dtype=jnp.int32)) % section_count]
    return out[None]


def solution(mesh):
    in_specs = (
        P(None, "dom", None),
        P(None, "dom", None, None),
        P(),
        P("section"),
        P("section", None, None, None),
    )
    out_specs = P("section", None, "dom", None)
    return jax.shard_map(local, mesh=mesh, in_specs=in_specs, out_specs=out_specs, check_vma=False)
```

profile of v0, /device:TPU:1, one launch (start us, length us, event | category | flops | bytes accessed | tf_op | source)
XLA Modules:
  0.0 214.7 jit_solution(17833681133331877498)
XLA Ops:
  0.0 3.6 %collective-permute-start.3 = (bf16[2,512,512]{2,1,0:T(8,128)(2,1)}, bf16[2,512,512]{2,1,0:T(8,128)(2,1)}, u32[]{:S(2)}, u32[]{:S(2)}) collective-permute-start(bf16[2,512,512]{2,1,0:T(8,128)(2,1)} %bitcast.102), channel_id=1, source_target_pairs={{0,64},{32,96},{64,0},{96,32},{1,65},{33,97},{65,1},{97,33},{2,66}... | collective-permute-start | bytes 3145736 | tf_op jit(solution)/shard_map/ppermute | solution.py:9
  7.2 8.3 %all-to-all-start.1 = ((bf16[32,64,512]{2,1,0:T(8,128)(2,1)}), bf16[32,64,512]{2,1,0:T(8,128)(2,1)}, u32[]{:S(2)}, u32[]{:S(2)}) async-start(bf16[32,64,512]{2,1,0:T(8,128)(2,1)} %gather_fusion.3), calls=%async_computation.1 | async-start | bytes 4194304 | tf_op jit(solution)/shard_map/all_to_all | solution.py:50
  15.6 2.9 %collective-permute-start = (s32[1]{0:T(128)}, s32[1]{0:T(128)}, u32[]{:S(2)}, u32[]{:S(2)}) collective-permute-start(s32[1]{0:T(128)} %param.10), channel_id=1, source_target_pairs={{0,32},{32,64},{64,96},{96,0},{1,33},{33,65},{65,97},{97,1},{2,34}... | collective-permute-start | bytes 20 | tf_op jit(solution)/shard_map/ppermute | solution.py:9
  19.8 6.6 %collective-permute-done.3 = bf16[2,512,512]{2,1,0:T(8,128)(2,1)} collective-permute-done((bf16[2,512,512]{2,1,0:T(8,128)(2,1)}, bf16[2,512,512]{2,1,0:T(8,128)(2,1)}, u32[]{:S(2)}, u32[]{:S(2)}) %collective-permute-start.3) | collective-permute-done | bytes 1048608 | tf_op jit(solution)/shard_map/ppermute | solution.py:9
  26.3 2.7 %pad_maximum_fusion.1 = bf16[2,2,512,512]{3,2,1,0:T(8,128)(2,1)} fusion(bf16[1,2,512,512]{3,2,1,0:T(8,128)(2,1)} %bitcast.23, bf16[1,2,512,512]{3,2,1,0:T(8,128)(2,1)S(1)} %copy-done.2), kind=kLoop, calls=%fused_computation.25 | loop fusion | flops 1048576 | bytes 4194304 | tf_op jit(solution)/shard_map/stack | solution.py:67
  29.1 2.9 %collective-permute-start.4 = (bf16[2,2,512,512]{3,2,1,0:T(8,128)(2,1)}, bf16[2,2,512,512]{3,2,1,0:T(8,128)(2,1)}, u32[]{:S(2)}, u32[]{:S(2)}) collective-permute-start(bf16[2,2,512,512]{3,2,1,0:T(8,128)(2,1)} %pad_maximum_fusion.1), channel_id=1, source_target_pairs={{0,32},{32,0},{64,96},{96,64},{1,33},{33,1},{65,97},{97,65},{2,34}... | collective-permute-start | bytes 6291464 | tf_op jit(solution)/shard_map/ppermute | solution.py:66
  37.9 10.3 %collective-permute-done = s32[1]{0:T(128)} collective-permute-done((s32[1]{0:T(128)}, s32[1]{0:T(128)}, u32[]{:S(2)}, u32[]{:S(2)}) %collective-permute-start) | collective-permute-done | bytes 36 | tf_op jit(solution)/shard_map/ppermute | solution.py:9
  59.4 2.1 convolution_bitcast_fusion
  64.6 3.2 %pad_maximum_fusion = bf16[4,2,512,512]{3,2,1,0:T(8,128)(2,1)} fusion(bf16[1,2,512,512]{3,2,1,0:T(8,128)(2,1)S(1)} %get-tuple-element.256, bf16[1,2,512,512]{3,2,1,0:T(8,128)(2,1)} %bitcast.23, bf16[1,2,512,512]{3,2,1,0:T(8,128)(2,1)S(1)} %get-tuple-element.255, bf16[1,2,512,512]{3,2,1,0:T(8,128)(2,1)S(1)} %copy-done.3), kind=kLoop, calls=%fused_computation.24 | loop fusion | flops 6291456 | bytes 8388608 | tf_op jit(solution)/shard_map/stack | solution.py:69
  67.9 130.5 %while.17 = (s32[]{:T(128)}, bf16[128,512]{1,0:T(8,128)(2,1)S(1)}, bf16[128,512]{0,1:T(8,128)(2,1)S(1)}, bf16[4,128,512]{2,1,0:T(8,128)(2,1)S(1)}, s32[]{:T(128)...) while((s32[]{:T(128)}, bf16[128,512]{1,0:T(8,128)(2,1)S(1)}, ...), condition=%wide.region_5.6_spmd, body=%wide.region_2.5_spmd.sunk | while | flops 353174784 | bytes 16554933 | solution.py:104
  73.2 2.0 gather_fusion
  75.2 9.2 %all-to-all-start = ((bf16[32,64,512]{2,1,0:T(8,128)(2,1)}), bf16[32,64,512]{2,1,0:T(8,128)(2,1)}, u32[]{:S(2)}, u32[]{:S(2)}) async-start(bf16[32,64,512]{2,1,0:T(8,128)(2,1)} %gather_fusion), calls=%async_computation | async-start | bytes 4194304 | tf_op jit(solution)/shard_map/while/body/all_to_all | solution.py:50
  84.8 28.0 %all-to-all-done = bf16[32,64,512]{2,1,0:T(8,128)(2,1)} async-done(((bf16[32,64,512]{2,1,0:T(8,128)(2,1)}), bf16[32,64,512]{2,1,0:T(8,128)(2,1)}, u32[]{:S(2)}, u32[]{:S(2)}) %all-to-all-start) | async-done | bytes 2097184 | tf_op jit(solution)/shard_map/while/body/all_to_all | solution.py:50
  112.8 2.4 %multiply_reduce_fusion.3 = (f32[128]{0:T(128)S(1)}, f32[512,128]{1,0:T(8,128)S(1)}) fusion(f32[512,128]{1,0:T(8,128)S(1)} %fusion.54, bf16[2048,512]{1,0:T(8,128)(2,1)} %bitcast.98, bf16[2048,128]{1,0:T(8,128)(2,1)} %get-tuple-element.388), kind=kOutput, calls=%fused_computation.14.clone.1 | convolution fusion | flops 268631936 | bytes 3146240 | tf_op jit(solution)/shard_map/while/body/kb,kd->bd/dot_general | solution.py:53
  120.5 2.0 gather_fusion
  122.6 5.0 %all-to-all-start = ((bf16[32,64,512]{2,1,0:T(8,128)(2,1)}), bf16[32,64,512]{2,1,0:T(8,128)(2,1)}, u32[]{:S(2)}, u32[]{:S(2)}) async-start(bf16[32,64,512]{2,1,0:T(8,128)(2,1)} %gather_fusion), calls=%async_computation | async-start | bytes 4194304 | tf_op jit(solution)/shard_map/while/body/all_to_all | solution.py:50
  128.0 26.6 %all-to-all-done = bf16[32,64,512]{2,1,0:T(8,128)(2,1)} async-done(((bf16[32,64,512]{2,1,0:T(8,128)(2,1)}), bf16[32,64,512]{2,1,0:T(8,128)(2,1)}, u32[]{:S(2)}, u32[]{:S(2)}) %all-to-all-start) | async-done | bytes 2097184 | tf_op jit(solution)/shard_map/while/body/all_to_all | solution.py:50
  154.6 2.4 %multiply_reduce_fusion.3 = (f32[128]{0:T(128)S(1)}, f32[512,128]{1,0:T(8,128)S(1)}) fusion(f32[512,128]{1,0:T(8,128)S(1)} %fusion.54, bf16[2048,512]{1,0:T(8,128)(2,1)} %bitcast.98, bf16[2048,128]{1,0:T(8,128)(2,1)} %get-tuple-element.388), kind=kOutput, calls=%fused_computation.14.clone.1 | convolution fusion | flops 268631936 | bytes 3146240 | tf_op jit(solution)/shard_map/while/body/kb,kd->bd/dot_general | solution.py:53
  162.3 2.0 gather_fusion
  164.4 5.3 %all-to-all-start = ((bf16[32,64,512]{2,1,0:T(8,128)(2,1)}), bf16[32,64,512]{2,1,0:T(8,128)(2,1)}, u32[]{:S(2)}, u32[]{:S(2)}) async-start(bf16[32,64,512]{2,1,0:T(8,128)(2,1)} %gather_fusion), calls=%async_computation | async-start | bytes 4194304 | tf_op jit(solution)/shard_map/while/body/all_to_all | solution.py:50
  170.1 25.9 %all-to-all-done = bf16[32,64,512]{2,1,0:T(8,128)(2,1)} async-done(((bf16[32,64,512]{2,1,0:T(8,128)(2,1)}), bf16[32,64,512]{2,1,0:T(8,128)(2,1)}, u32[]{:S(2)}, u32[]{:S(2)}) %all-to-all-start) | async-done | bytes 2097184 | tf_op jit(solution)/shard_map/while/body/all_to_all | solution.py:50
  195.9 2.4 %multiply_reduce_fusion.3 = (f32[128]{0:T(128)S(1)}, f32[512,128]{1,0:T(8,128)S(1)}) fusion(f32[512,128]{1,0:T(8,128)S(1)} %fusion.54, bf16[2048,512]{1,0:T(8,128)(2,1)} %bitcast.98, bf16[2048,128]{1,0:T(8,128)(2,1)} %get-tuple-element.388), kind=kOutput, calls=%fused_computation.14.clone.1 | convolution fusion | flops 268631936 | bytes 3146240 | tf_op jit(solution)/shard_map/while/body/kb,kd->bd/dot_general | solution.py:53
  199.9 5.7 %collective-permute-start.5 = (bf16[128,512]{1,0:T(8,128)(2,1)S(1)}, bf16[128,512]{1,0:T(8,128)(2,1)S(1)}, u32[]{:S(2)}, u32[]{:S(2)}) collective-permute-start(bf16[128,512]{1,0:T(8,128)(2,1)S(1)} %get-tuple-element.260), channel_id=1, source_target_pairs={{0,32},{32,64},{64,96},{96,0},{1,33},{33,65},{65,97},{97,1},{2,34}... | collective-permute-start | bytes 393224 | tf_op jit(solution)/shard_map/ppermute | solution.py:9
  208.2 4.3 %collective-permute-done.6 = bf16[128,512]{1,0:T(8,128)(2,1)S(1)} collective-permute-done((bf16[128,512]{1,0:T(8,128)(2,1)S(1)}, bf16[128,512]{1,0:T(8,128)(2,1)S(1)}, u32[]{:S(2)}, u32[]{:S(2)}) %collective-permute-start.6) | collective-permute-done | bytes 131104 | tf_op jit(solution)/shard_map/ppermute | solution.py:9
  (91 shorter events, 38.4 us)
Async XLA Ops:
  0.0 19.7 %copy-start = (bf16[4,2,64,2112]{3,2,1,0:T(8,128)(2,1)S(1)}, bf16[4,2,64,2112]{3,2,1,0:T(8,128)(2,1)}, u32[]{:S(2)}) copy-start(bf16[4,2,64,2112]{3,2,1,0:T(8,128)(2,1)} %param.8) | copy-start | bytes 6488068
  0.0 26.3 %collective-permute-start.3 = (bf16[2,512,512]{2,1,0:T(8,128)(2,1)}, bf16[2,512,512]{2,1,0:T(8,128)(2,1)}, u32[]{:S(2)}, u32[]{:S(2)}) collective-permute-start(bf16[2,512,512]{2,1,0:T(8,128)(2,1)} %bitcast.102), channel_id=1, source_target_pairs={{0,64},{32,96},{64,0},{96,32},{1,65},{33,97},{65,1},{97,33},{2,66}... | collective-permute-start | bytes 3145736 | tf_op jit(solution)/shard_map/ppermute | solution.py:9
  7.2 19.1 %copy-start.2 = (bf16[1,2,512,512]{3,2,1,0:T(8,128)(2,1)S(1)}, bf16[1,2,512,512]{3,2,1,0:T(8,128)(2,1)}, u32[]{:S(2)}) copy-start(bf16[1,2,512,512]{3,2,1,0:T(8,128)(2,1)} %param.11) | copy-start | bytes 3145732
  7.2 52.2 %all-to-all-start.1 = ((bf16[32,64,512]{2,1,0:T(8,128)(2,1)}), bf16[32,64,512]{2,1,0:T(8,128)(2,1)}, u32[]{:S(2)}, u32[]{:S(2)}) async-start(bf16[32,64,512]{2,1,0:T(8,128)(2,1)} %gather_fusion.3), calls=%async_computation.1 | async-start | bytes 4194304 | tf_op jit(solution)/shard_map/all_to_all | solution.py:50
  15.6 32.7 %collective-permute-start = (s32[1]{0:T(128)}, s32[1]{0:T(128)}, u32[]{:S(2)}, u32[]{:S(2)}) collective-permute-start(s32[1]{0:T(128)} %param.10), channel_id=1, source_target_pairs={{0,32},{32,64},{64,96},{96,0},{1,33},{33,65},{65,97},{97,1},{2,34}... | collective-permute-start | bytes 20 | tf_op jit(solution)/shard_map/ppermute | solution.py:9
  18.5 30.0 %collective-permute-start.1 = (s32[1]{0:T(128)}, s32[1]{0:T(128)}, u32[]{:S(2)}, u32[]{:S(2)}) collective-permute-start(s32[1]{0:T(128)} %param.10), channel_id=1, source_target_pairs={{0,64},{32,96},{64,0},{96,32},{1,65},{33,97},{65,1},{97,33},{2,66}... | collective-permute-start | bytes 20 | tf_op jit(solution)/shard_map/ppermute | solution.py:9
  19.7 30.4 %collective-permute-start.2 = (s32[1]{0:T(128)}, s32[1]{0:T(128)}, u32[]{:S(2)}, u32[]{:S(2)}) collective-permute-start(s32[1]{0:T(128)} %param.10), channel_id=1, source_target_pairs={{0,96},{32,0},{64,32},{96,64},{1,97},{33,1},{65,33},{97,65},{2,98}... | collective-permute-start | bytes 20 | tf_op jit(solution)/shard_map/ppermute | solution.py:9
  19.8 12.3 %copy-start.4 = (bf16[1,2,64,2112]{3,2,1,0:T(8,128)(2,1)}, bf16[1,2,64,2112]{3,2,1,0:T(8,128)(2,1)S(1)}, u32[]{:S(2)}) copy-start(bf16[1,2,64,2112]{3,2,1,0:T(8,128)(2,1)S(1)} %constant_dynamic-slice_fusion.3) | copy-start | bytes 1622020
  29.1 33.7 %collective-permute-start.4 = (bf16[2,2,512,512]{3,2,1,0:T(8,128)(2,1)}, bf16[2,2,512,512]{3,2,1,0:T(8,128)(2,1)}, u32[]{:S(2)}, u32[]{:S(2)}) collective-permute-start(bf16[2,2,512,512]{3,2,1,0:T(8,128)(2,1)} %pad_maximum_fusion.1), channel_id=1, source_target_pairs={{0,32},{32,0},{64,96},{96,64},{1,33},{33,1},{65,97},{97,65},{2,34}... | collective-permute-start | bytes 6291464 | tf_op jit(solution)/shard_map/ppermute | solution.py:66
  36.2 26.3 %copy-start.1 = (bf16[32,64,128]{2,1,0:T(8,128)(2,1)}, bf16[32,64,128]{2,1,0:T(8,128)(2,1)S(1)}, u32[]{:S(2)}) copy-start(bf16[32,64,128]{2,1,0:T(8,128)(2,1)S(1)} %gather_fusion.2) | copy-start | bytes 1572868
  62.8 1.9 copy-start.3
  64.6 3.3 %copy-start.5 = (bf16[128,128]{1,0:T(8,128)(2,1)S(1)}, bf16[128,128]{1,0:T(8,128)(2,1)}, u32[]{:S(2)}) copy-start(bf16[128,128]{1,0:T(8,128)(2,1)} %copy.12) | copy-start | bytes 98308
  75.2 37.6 %all-to-all-start = ((bf16[32,64,512]{2,1,0:T(8,128)(2,1)}), bf16[32,64,512]{2,1,0:T(8,128)(2,1)}, u32[]{:S(2)}, u32[]{:S(2)}) async-start(bf16[32,64,512]{2,1,0:T(8,128)(2,1)} %gather_fusion), calls=%async_computation | async-start | bytes 4194304 | tf_op jit(solution)/shard_map/while/body/all_to_all | solution.py:50
  122.6 32.0 %all-to-all-start = ((bf16[32,64,512]{2,1,0:T(8,128)(2,1)}), bf16[32,64,512]{2,1,0:T(8,128)(2,1)}, u32[]{:S(2)}, u32[]{:S(2)}) async-start(bf16[32,64,512]{2,1,0:T(8,128)(2,1)} %gather_fusion), calls=%async_computation | async-start | bytes 4194304 | tf_op jit(solution)/shard_map/while/body/all_to_all | solution.py:50
  164.4 31.5 %all-to-all-start = ((bf16[32,64,512]{2,1,0:T(8,128)(2,1)}), bf16[32,64,512]{2,1,0:T(8,128)(2,1)}, u32[]{:S(2)}, u32[]{:S(2)}) async-start(bf16[32,64,512]{2,1,0:T(8,128)(2,1)} %gather_fusion), calls=%async_computation | async-start | bytes 4194304 | tf_op jit(solution)/shard_map/while/body/all_to_all | solution.py:50
  199.9 8.4 %collective-permute-start.5 = (bf16[128,512]{1,0:T(8,128)(2,1)S(1)}, bf16[128,512]{1,0:T(8,128)(2,1)S(1)}, u32[]{:S(2)}, u32[]{:S(2)}) collective-permute-start(bf16[128,512]{1,0:T(8,128)(2,1)S(1)} %get-tuple-element.260), channel_id=1, source_target_pairs={{0,32},{32,64},{64,96},{96,0},{1,33},{33,65},{65,97},{97,1},{2,34}... | collective-permute-start | bytes 393224 | tf_op jit(solution)/shard_map/ppermute | solution.py:9
  205.6 7.0 %collective-permute-start.6 = (bf16[128,512]{1,0:T(8,128)(2,1)S(1)}, bf16[128,512]{1,0:T(8,128)(2,1)S(1)}, u32[]{:S(2)}, u32[]{:S(2)}) collective-permute-start(bf16[128,512]{1,0:T(8,128)(2,1)S(1)} %get-tuple-element.259), channel_id=1, source_target_pairs={{0,64},{32,96},{64,0},{96,32},{1,65},{33,97},{65,1},{97,33},{2,66}... | collective-permute-start | bytes 393224 | tf_op jit(solution)/shard_map/ppermute | solution.py:9
  206.7 6.6 %collective-permute-start.7 = (bf16[128,512]{1,0:T(8,128)(2,1)S(1)}, bf16[128,512]{1,0:T(8,128)(2,1)S(1)}, u32[]{:S(2)}, u32[]{:S(2)}) collective-permute-start(bf16[128,512]{1,0:T(8,128)(2,1)S(1)} %get-tuple-element.258), channel_id=1, source_target_pairs={{0,96},{32,0},{64,32},{96,64},{1,97},{33,1},{65,33},{97,65},{2,98}... | collective-permute-start | bytes 393224 | tf_op jit(solution)/shard_map/ppermute | solution.py:9
where the time goes:
time: 216 us; the launch traced here: 215 us
  waiting for transfers between devices  106 us (49%)
  starting transfers between devices  45.4 us (21%)
  local copies, waits for them, and re-layouts  23.8 us (11%)
  matrix products  16.3 us (8%)
  other arithmetic  13.2 us (6%)
  loops' own time  6.13 us (3%)
  between operations  4.17 us (2%)
    all_to_all x4, waiting for transfers between devices, normed_of(): incoming = lax.all_to_all(outgoing, 'dom', 0, 0, tiled=True)  80.4 us
    all_to_all x4, starting transfers between devices, normed_of(): incoming = lax.all_to_all(outgoing, 'dom', 0, 0, tiled=True)  27.9 us
    ppermute x7, waiting for transfers between devices, shifted(): lax.ppermute(value, axis, [(source, (source + steps) % count) for source...  25.3 us
    ppermute x7, starting transfers between devices, shifted(): lax.ppermute(value, axis, [(source, (source + steps) % count) for source...  14.6 us
    dot_general x4, matrix products, normed_of(): jnp.einsum('kb,kd->bd', adj_t_by_part, incoming.reshape(-1, feature_width...  9.36 us
    gather x4, local copies, waits for them, and re-layouts, normed_of(): outgoing = local_view[send_ids]  8.08 us
    another operation x1, loops' own time, local(): lax.fori_loop(0, jnp.maximum(total - 1, 0), layer_step, (hidden, normed,...  6.13 us
    dot_general x4, matrix products, projected_onto(): projected = jnp.dot(normed, weight, preferred_element_type=jnp.float32)  5.31 us
  transfers between devices with their start and end apart: 12, of which 10 were waited for; matrix products, arithmetic and copies ran while one was open for 10% of the time, Pallas kernels for 0%

commit v1 on v0

--- a/solution.py
+++ b/solution.py
@@ -61,12 +61,17 @@
         projected = jnp.dot(normed, weight, preferred_element_type=jnp.float32)
         return (hidden.astype(jnp.float32) + jax.nn.relu(projected)).astype(jnp.bfloat16)
 
-    if section_count == 4:
-        across = shifted(weights[0], "section", 2)
-        beside = lax.ppermute(
-            jnp.stack([weights[0], across]), "section", [(0, 1), (1, 0), (2, 3), (3, 2)]
-        )
-        weight_list = jnp.stack([weights[0], beside[0], across, beside[1]])
+    if section_count == 4 and part_count % 2 == 0:
+        pairs = [
+            (section * part_count + part, (section ^ 2) * part_count + (part ^ 1))
+            for section in range(section_count)
+            for part in range(part_count)
+        ]
+        across = lax.ppermute(weights[0], ("section", "dom"), pairs)
+        core_swap = [(0, 1), (1, 0), (2, 3), (3, 2)]
+        beside_own = lax.ppermute(weights[0], "section", core_swap)
+        beside_far = lax.ppermute(across, "section", core_swap)
+        weight_list = jnp.stack([weights[0], beside_own, across, beside_far])
 
         def list_index(section):
             return jnp.bitwise_xor(section, group)

time: 216 us -> 205 us (0.949)
  waiting for transfers between devices: 106 us -> 101 us
  other arithmetic: 13.2 us -> 10.9 us
  starting transfers between devices: 45.4 us -> 43.1 us
    ppermute x7 -> x6, waiting for transfers between devices: 25.3 us -> 18.5 us  [shifted(): lax.ppermute(value, axis, [(source, (source + steps) % count) for source...]
    ppermute x7 -> x6, starting transfers between devices: 14.6 us -> 10.4 us  [shifted(): lax.ppermute(value, axis, [(source, (source + steps) % count) for source...]
    another operation x3 -> x2, other arithmetic: 6.16 us -> 3.88 us  [the longest x1 3.7 us: local(): weight_list = jnp.stack([weights[0], beside_own, across, beside_far])]
    all_to_all x4, waiting for transfers between devices: 80.4 us -> 82.7 us  [normed_of(): incoming = lax.all_to_all(outgoing, 'dom', 0, 0, tiled=True)]
    ppermute x1 -> x3, starting transfers between devices: 2.89 us -> 4.83 us  [the longest x1 2.7 us: local(): across = lax.ppermute(weights[0], ('section', 'dom'), pairs)]
  transfers between devices with their start and end apart: 12 -> 13, of which waited for: 10 -> 9; matrix products, arithmetic and copies ran while one was open for 10% -> 8% of each run, Pallas kernels for 0% -> 0%
where the time goes in v1:
time: 205 us; the launch traced here: 204 us
  waiting for transfers between devices  101 us (49%)
  starting transfers between devices  43.1 us (21%)
  local copies, waits for them, and re-layouts  22.6 us (11%)
  matrix products  16.3 us (8%)
  other arithmetic  10.9 us (5%)
  loops' own time  5.76 us (3%)
  between operations  4.19 us (2%)
    all_to_all x4, waiting for transfers between devices, normed_of(): incoming = lax.all_to_all(outgoing, 'dom', 0, 0, tiled=True)  82.7 us
    all_to_all x4, starting transfers between devices, normed_of(): incoming = lax.all_to_all(outgoing, 'dom', 0, 0, tiled=True)  27.8 us
    ppermute x6, waiting for transfers between devices, shifted(): lax.ppermute(value, axis, [(source, (source + steps) % count) for source...  18.5 us
    ppermute x6, starting transfers between devices, shifted(): lax.ppermute(value, axis, [(source, (source + steps) % count) for source...  10.4 us
    dot_general x4, matrix products, normed_of(): jnp.einsum('kb,kd->bd', adj_t_by_part, incoming.reshape(-1, feature_width...  9.36 us
    gather x4, local copies, waits for them, and re-layouts, normed_of(): outgoing = local_view[send_ids]  8.09 us
    another operation x1, loops' own time, local(): lax.fori_loop(0, jnp.maximum(total - 1, 0), layer_step, (hidden, normed,...  5.76 us
    dot_general x4, matrix products, projected_onto(): projected = jnp.dot(normed, weight, preferred_element_type=jnp.float32)  5.31 us
  transfers between devices with their start and end apart: 13, of which 9 were waited for; matrix products, arithmetic and copies ran while one was open for 8% of the time, Pallas kernels for 0%

profile of v1, /device:TPU:1, one launch (start us, length us, event | category | flops | bytes accessed | tf_op | source)
XLA Modules:
  0.0 204.0 jit_solution(13111472968327420916)
XLA Ops:
  1.8 2.0 gather_fusion.3
  3.8 9.9 %all-to-all-start.1 = ((bf16[32,64,512]{2,1,0:T(8,128)(2,1)}), bf16[32,64,512]{2,1,0:T(8,128)(2,1)}, u32[]{:S(2)}, u32[]{:S(2)}) async-start(bf16[32,64,512]{2,1,0:T(8,128)(2,1)} %gather_fusion.3), calls=%async_computation.1 | async-start | bytes 4194304 | tf_op jit(solution)/shard_map/all_to_all | solution.py:50
  13.7 3.4 %collective-permute-start = (s32[1]{0:T(128)}, s32[1]{0:T(128)}, u32[]{:S(2)}, u32[]{:S(2)}) collective-permute-start(s32[1]{0:T(128)} %param.10), channel_id=1, source_target_pairs={{0,32},{32,64},{64,96},{96,0},{1,33},{33,65},{65,97},{97,1},{2,34}... | collective-permute-start | bytes 20 | tf_op jit(solution)/shard_map/ppermute | solution.py:9
  17.6 2.7 %collective-permute-start.4 = (bf16[2,512,512]{2,1,0:T(8,128)(2,1)}, bf16[2,512,512]{2,1,0:T(8,128)(2,1)}, u32[]{:S(2)}, u32[]{:S(2)}) collective-permute-start(bf16[2,512,512]{2,1,0:T(8,128)(2,1)} %bitcast.22), channel_id=1, source_target_pairs={{0,65},{1,64},{2,67},{3,66},{4,69},{5,68},{6,71},{7,70},{8,73},{9,... | collective-permute-start | bytes 3145736 | tf_op jit(solution)/shard_map/ppermute | solution.py:70
  28.8 7.6 %collective-permute-done = s32[1]{0:T(128)} collective-permute-done((s32[1]{0:T(128)}, s32[1]{0:T(128)}, u32[]{:S(2)}, u32[]{:S(2)}) %collective-permute-start) | collective-permute-done | bytes 36 | tf_op jit(solution)/shard_map/ppermute | solution.py:9
  36.4 3.2 %collective-permute-done.1 = s32[1]{0:T(128)} collective-permute-done((s32[1]{0:T(128)}, s32[1]{0:T(128)}, u32[]{:S(2)}, u32[]{:S(2)}) %collective-permute-start.1) | collective-permute-done | bytes 36 | tf_op jit(solution)/shard_map/ppermute | solution.py:9
  40.8 2.0 pad_add_fusion
  50.5 2.1 %convolution_bitcast_fusion = f32[128,512]{1,0:T(8,128)S(1)} fusion(bf16[32,64,128]{2,1,0:T(8,128)(2,1)S(1)} %gather_fusion.2, bf16[32,64,512]{2,1,0:T(8,128)(2,1)} %all-to-all-done.1), kind=kOutput, calls=%fused_computation.26 | convolution fusion | flops 268435456 | bytes 2883584 | tf_op jit(solution)/shard_map/kb,kd->bd/dot_general | solution.py:53
  53.8 3.7 %pad_maximum_fusion = bf16[4,2,512,512]{3,2,1,0:T(8,128)(2,1)} fusion(bf16[1,2,512,512]{3,2,1,0:T(8,128)(2,1)} %bitcast.25, bf16[1,2,512,512]{3,2,1,0:T(8,128)(2,1)} %bitcast.24, bf16[1,2,512,512]{3,2,1,0:T(8,128)(2,1)} %bitcast.23, bf16[1,2,512,512]{3,2,1,0:T(8,128)(2,1)} %param.11), kind=kLoop, calls=%fused_computation.24 | loop fusion | flops 6291456 | bytes 8388608 | tf_op jit(solution)/shard_map/stack | solution.py:74
  57.6 130.4 %while.17 = (s32[]{:T(128)}, bf16[128,512]{1,0:T(8,128)(2,1)S(1)}, bf16[128,512]{0,1:T(8,128)(2,1)S(1)}, bf16[4,128,512]{2,1,0:T(8,128)(2,1)S(1)}, s32[]{:T(128)...) while((s32[]{:T(128)}, bf16[128,512]{1,0:T(8,128)(2,1)S(1)}, ...), condition=%wide.region_5.6_spmd, body=%wide.region_2.5_spmd.sunk | while | flops 353174784 | bytes 16554933 | solution.py:109
  62.6 2.0 gather_fusion
  64.7 7.1 %all-to-all-start = ((bf16[32,64,512]{2,1,0:T(8,128)(2,1)}), bf16[32,64,512]{2,1,0:T(8,128)(2,1)}, u32[]{:S(2)}, u32[]{:S(2)}) async-start(bf16[32,64,512]{2,1,0:T(8,128)(2,1)} %gather_fusion), calls=%async_computation | async-start | bytes 4194304 | tf_op jit(solution)/shard_map/while/body/all_to_all | solution.py:50
  72.1 28.8 %all-to-all-done = bf16[32,64,512]{2,1,0:T(8,128)(2,1)} async-done(((bf16[32,64,512]{2,1,0:T(8,128)(2,1)}), bf16[32,64,512]{2,1,0:T(8,128)(2,1)}, u32[]{:S(2)}, u32[]{:S(2)}) %all-to-all-start) | async-done | bytes 2097184 | tf_op jit(solution)/shard_map/while/body/all_to_all | solution.py:50
  100.9 2.4 %multiply_reduce_fusion.3 = (f32[128]{0:T(128)S(1)}, f32[512,128]{1,0:T(8,128)S(1)}) fusion(f32[512,128]{1,0:T(8,128)S(1)} %fusion.53, bf16[2048,512]{1,0:T(8,128)(2,1)} %bitcast.100, bf16[2048,128]{1,0:T(8,128)(2,1)} %get-tuple-element.386), kind=kOutput, calls=%fused_computation.14.clone.1 | convolution fusion | flops 268631936 | bytes 3146240 | tf_op jit(solution)/shard_map/while/body/kb,kd->bd/dot_general | solution.py:53
  108.4 2.0 gather_fusion
  110.5 6.1 %all-to-all-start = ((bf16[32,64,512]{2,1,0:T(8,128)(2,1)}), bf16[32,64,512]{2,1,0:T(8,128)(2,1)}, u32[]{:S(2)}, u32[]{:S(2)}) async-start(bf16[32,64,512]{2,1,0:T(8,128)(2,1)} %gather_fusion), calls=%async_computation | async-start | bytes 4194304 | tf_op jit(solution)/shard_map/while/body/all_to_all | solution.py:50
  116.9 27.6 %all-to-all-done = bf16[32,64,512]{2,1,0:T(8,128)(2,1)} async-done(((bf16[32,64,512]{2,1,0:T(8,128)(2,1)}), bf16[32,64,512]{2,1,0:T(8,128)(2,1)}, u32[]{:S(2)}, u32[]{:S(2)}) %all-to-all-start) | async-done | bytes 2097184 | tf_op jit(solution)/shard_map/while/body/all_to_all | solution.py:50
  144.5 2.4 %multiply_reduce_fusion.3 = (f32[128]{0:T(128)S(1)}, f32[512,128]{1,0:T(8,128)S(1)}) fusion(f32[512,128]{1,0:T(8,128)S(1)} %fusion.53, bf16[2048,512]{1,0:T(8,128)(2,1)} %bitcast.100, bf16[2048,128]{1,0:T(8,128)(2,1)} %get-tuple-element.386), kind=kOutput, calls=%fused_computation.14.clone.1 | convolution fusion | flops 268631936 | bytes 3146240 | tf_op jit(solution)/shard_map/while/body/kb,kd->bd/dot_general | solution.py:53
  152.0 2.0 gather_fusion
  154.1 4.8 %all-to-all-start = ((bf16[32,64,512]{2,1,0:T(8,128)(2,1)}), bf16[32,64,512]{2,1,0:T(8,128)(2,1)}, u32[]{:S(2)}, u32[]{:S(2)}) async-start(bf16[32,64,512]{2,1,0:T(8,128)(2,1)} %gather_fusion), calls=%async_computation | async-start | bytes 4194304 | tf_op jit(solution)/shard_map/while/body/all_to_all | solution.py:50
  159.2 26.3 %all-to-all-done = bf16[32,64,512]{2,1,0:T(8,128)(2,1)} async-done(((bf16[32,64,512]{2,1,0:T(8,128)(2,1)}), bf16[32,64,512]{2,1,0:T(8,128)(2,1)}, u32[]{:S(2)}, u32[]{:S(2)}) %all-to-all-start) | async-done | bytes 2097184 | tf_op jit(solution)/shard_map/while/body/all_to_all | solution.py:50
  185.5 2.4 %multiply_reduce_fusion.3 = (f32[128]{0:T(128)S(1)}, f32[512,128]{1,0:T(8,128)S(1)}) fusion(f32[512,128]{1,0:T(8,128)S(1)} %fusion.53, bf16[2048,512]{1,0:T(8,128)(2,1)} %bitcast.100, bf16[2048,128]{1,0:T(8,128)(2,1)} %get-tuple-element.386), kind=kOutput, calls=%fused_computation.14.clone.1 | convolution fusion | flops 268631936 | bytes 3146240 | tf_op jit(solution)/shard_map/while/body/kb,kd->bd/dot_general | solution.py:53
  189.5 5.7 %collective-permute-start.6 = (bf16[128,512]{1,0:T(8,128)(2,1)S(1)}, bf16[128,512]{1,0:T(8,128)(2,1)S(1)}, u32[]{:S(2)}, u32[]{:S(2)}) collective-permute-start(bf16[128,512]{1,0:T(8,128)(2,1)S(1)} %get-tuple-element.258), channel_id=1, source_target_pairs={{0,32},{32,64},{64,96},{96,0},{1,33},{33,65},{65,97},{97,1},{2,34}... | collective-permute-start | bytes 393224 | tf_op jit(solution)/shard_map/ppermute | solution.py:9
  197.8 4.0 %collective-permute-done.7 = bf16[128,512]{1,0:T(8,128)(2,1)S(1)} collective-permute-done((bf16[128,512]{1,0:T(8,128)(2,1)S(1)}, bf16[128,512]{1,0:T(8,128)(2,1)S(1)}, u32[]{:S(2)}, u32[]{:S(2)}) %collective-permute-start.7) | collective-permute-done | bytes 131104 | tf_op jit(solution)/shard_map/ppermute | solution.py:9
  (87 shorter events, 33.8 us)
Async XLA Ops:
  0.0 22.1 %copy-start = (bf16[4,2,64,2112]{3,2,1,0:T(8,128)(2,1)S(1)}, bf16[4,2,64,2112]{3,2,1,0:T(8,128)(2,1)}, u32[]{:S(2)}) copy-start(bf16[4,2,64,2112]{3,2,1,0:T(8,128)(2,1)} %param.8) | copy-start | bytes 6488068
  3.8 46.7 %all-to-all-start.1 = ((bf16[32,64,512]{2,1,0:T(8,128)(2,1)}), bf16[32,64,512]{2,1,0:T(8,128)(2,1)}, u32[]{:S(2)}, u32[]{:S(2)}) async-start(bf16[32,64,512]{2,1,0:T(8,128)(2,1)} %gather_fusion.3), calls=%async_computation.1 | async-start | bytes 4194304 | tf_op jit(solution)/shard_map/all_to_all | solution.py:50
  13.7 22.7 %collective-permute-start = (s32[1]{0:T(128)}, s32[1]{0:T(128)}, u32[]{:S(2)}, u32[]{:S(2)}) collective-permute-start(s32[1]{0:T(128)} %param.10), channel_id=1, source_target_pairs={{0,32},{32,64},{64,96},{96,0},{1,33},{33,65},{65,97},{97,1},{2,34}... | collective-permute-start | bytes 20 | tf_op jit(solution)/shard_map/ppermute | solution.py:9
  17.1 22.6 %collective-permute-start.1 = (s32[1]{0:T(128)}, s32[1]{0:T(128)}, u32[]{:S(2)}, u32[]{:S(2)}) collective-permute-start(s32[1]{0:T(128)} %param.10), channel_id=1, source_target_pairs={{0,64},{32,96},{64,0},{96,32},{1,65},{33,97},{65,1},{97,33},{2,66}... | collective-permute-start | bytes 20 | tf_op jit(solution)/shard_map/ppermute | solution.py:9
  17.6 23.2 %collective-permute-start.2 = (s32[1]{0:T(128)}, s32[1]{0:T(128)}, u32[]{:S(2)}, u32[]{:S(2)}) collective-permute-start(s32[1]{0:T(128)} %param.10), channel_id=1, source_target_pairs={{0,96},{32,0},{64,32},{96,64},{1,97},{33,1},{65,33},{97,65},{2,98}... | collective-permute-start | bytes 20 | tf_op jit(solution)/shard_map/ppermute | solution.py:9
  17.6 28.1 %collective-permute-start.4 = (bf16[2,512,512]{2,1,0:T(8,128)(2,1)}, bf16[2,512,512]{2,1,0:T(8,128)(2,1)}, u32[]{:S(2)}, u32[]{:S(2)}) collective-permute-start(bf16[2,512,512]{2,1,0:T(8,128)(2,1)} %bitcast.22), channel_id=1, source_target_pairs={{0,65},{1,64},{2,67},{3,66},{4,69},{5,68},{6,71},{7,70},{8,73},{9,... | collective-permute-start | bytes 3145736 | tf_op jit(solution)/shard_map/ppermute | solution.py:70
  20.3 33.5 %collective-permute-start.3 = (bf16[2,512,512]{2,1,0:T(8,128)(2,1)}, bf16[2,512,512]{2,1,0:T(8,128)(2,1)}, u32[]{:S(2)}, u32[]{:S(2)}) collective-permute-start(bf16[2,512,512]{2,1,0:T(8,128)(2,1)} %bitcast.22), channel_id=1, source_target_pairs={{0,32},{32,0},{64,96},{96,64},{1,33},{33,1},{65,97},{97,65},{2,34}... | collective-permute-start | bytes 3145736 | tf_op jit(solution)/shard_map/ppermute | solution.py:72
  22.1 0.8 copy-start.2
  27.1 26.5 %copy-start.1 = (bf16[32,64,128]{2,1,0:T(8,128)(2,1)}, bf16[32,64,128]{2,1,0:T(8,128)(2,1)S(1)}, u32[]{:S(2)}) copy-start(bf16[32,64,128]{2,1,0:T(8,128)(2,1)S(1)} %gather_fusion.2) | copy-start | bytes 1572868
  45.7 8.1 %collective-permute-start.5 = (bf16[2,512,512]{2,1,0:T(8,128)(2,1)}, bf16[2,512,512]{2,1,0:T(8,128)(2,1)}, u32[]{:S(2)}, u32[]{:S(2)}) collective-permute-start(bf16[2,512,512]{2,1,0:T(8,128)(2,1)} %collective-permute-done.4), channel_id=1, source_target_pairs={{0,32},{32,0},{64,96},{96,64},{1,33},{33,1},{65,97},{97,65},{2,34}... | collective-permute-start | bytes 3145736 | tf_op jit(solution)/shard_map/ppermute | solution.py:73
  53.8 3.8 %copy-start.3 = (bf16[128,128]{1,0:T(8,128)(2,1)S(1)}, bf16[128,128]{1,0:T(8,128)(2,1)}, u32[]{:S(2)}) copy-start(bf16[128,128]{1,0:T(8,128)(2,1)} %copy.12) | copy-start | bytes 98308
  64.7 36.2 %all-to-all-start = ((bf16[32,64,512]{2,1,0:T(8,128)(2,1)}), bf16[32,64,512]{2,1,0:T(8,128)(2,1)}, u32[]{:S(2)}, u32[]{:S(2)}) async-start(bf16[32,64,512]{2,1,0:T(8,128)(2,1)} %gather_fusion), calls=%async_computation | async-start | bytes 4194304 | tf_op jit(solution)/shard_map/while/body/all_to_all | solution.py:50
  110.5 34.1 %all-to-all-start = ((bf16[32,64,512]{2,1,0:T(8,128)(2,1)}), bf16[32,64,512]{2,1,0:T(8,128)(2,1)}, u32[]{:S(2)}, u32[]{:S(2)}) async-start(bf16[32,64,512]{2,1,0:T(8,128)(2,1)} %gather_fusion), calls=%async_computation | async-start | bytes 4194304 | tf_op jit(solution)/shard_map/while/body/all_to_all | solution.py:50
  154.1 31.4 %all-to-all-start = ((bf16[32,64,512]{2,1,0:T(8,128)(2,1)}), bf16[32,64,512]{2,1,0:T(8,128)(2,1)}, u32[]{:S(2)}, u32[]{:S(2)}) async-start(bf16[32,64,512]{2,1,0:T(8,128)(2,1)} %gather_fusion), calls=%async_computation | async-start | bytes 4194304 | tf_op jit(solution)/shard_map/while/body/all_to_all | solution.py:50
  189.5 8.4 %collective-permute-start.6 = (bf16[128,512]{1,0:T(8,128)(2,1)S(1)}, bf16[128,512]{1,0:T(8,128)(2,1)S(1)}, u32[]{:S(2)}, u32[]{:S(2)}) collective-permute-start(bf16[128,512]{1,0:T(8,128)(2,1)S(1)} %get-tuple-element.258), channel_id=1, source_target_pairs={{0,32},{32,64},{64,96},{96,0},{1,33},{33,65},{65,97},{97,1},{2,34}... | collective-permute-start | bytes 393224 | tf_op jit(solution)/shard_map/ppermute | solution.py:9
  195.2 6.6 %collective-permute-start.7 = (bf16[128,512]{1,0:T(8,128)(2,1)S(1)}, bf16[128,512]{1,0:T(8,128)(2,1)S(1)}, u32[]{:S(2)}, u32[]{:S(2)}) collective-permute-start(bf16[128,512]{1,0:T(8,128)(2,1)S(1)} %get-tuple-element.257), channel_id=1, source_target_pairs={{0,64},{32,96},{64,0},{96,32},{1,65},{33,97},{65,1},{97,33},{2,66}... | collective-permute-start | bytes 393224 | tf_op jit(solution)/shard_map/ppermute | solution.py:9
  196.0 6.6 %collective-permute-start.8 = (bf16[128,512]{1,0:T(8,128)(2,1)S(1)}, bf16[128,512]{1,0:T(8,128)(2,1)S(1)}, u32[]{:S(2)}, u32[]{:S(2)}) collective-permute-start(bf16[128,512]{1,0:T(8,128)(2,1)S(1)} %get-tuple-element.256), channel_id=1, source_target_pairs={{0,96},{32,0},{64,32},{96,64},{1,97},{33,1},{65,33},{97,65},{2,98}... | collective-permute-start | bytes 393224 | tf_op jit(solution)/shard_map/ppermute | solution.py:9
